TPU v7x, 256 devices: a whole 4x4x8 slice. The times are simulated.
256 devices in a mesh: dp: 16 (over z, core), tensor: 16 (over y, x).
Axes of the slice: x: 4, y: 4, z: 8, core: 2. Of those that a mesh axis runs over, the one named last changes fastest.
Arguments:
- tokens: bfloat16 [8192, 2048], P(('dp', 'tensor')), may hold values from -6 to 6
- lengths: int32 [16, 8], P('dp'), may hold values from 1 to 128, 512 in all within a row
- group_prefix: int32 [16], replicated, may hold values from 0 to 15, as said below
- prefix_cache: bfloat16 [65536, 512], P(('dp', 'tensor')), may hold values from -340 to 340
- query_weight: bfloat16 [2048, 1024], P(None, 'tensor'), may hold values from -0.125 to 0.125
- key_weight: bfloat16 [2048, 256], replicated, may hold values from -0.375 to 0.375
- value_weight: bfloat16 [2048, 256], replicated, may hold values from -0.125 to 0.125
- out_weight: bfloat16 [1024, 2048], P('tensor'), may hold values from -0.1875 to 0.1875
- gate_up_weight: bfloat16 [2, 2048, 5120], P(None, None, 'tensor'), may hold values from -0.125 to 0.125
- down_weight: bfloat16 [5120, 2048], P('tensor'), may hold values from -0.078125 to 0.078125
Outputs:
- layer_out: bfloat16 [8192, 2048], P(('dp', 'tensor'))
Inputs may be any that keep to these rules, and one draw needn't show every extreme that they name: The 8 lengths of a group sum to 512, and one of them is exactly 128. `group_prefix`: several groups may continue the same slot.
All inputs are finite; a program needn't handle non-finite values.
Results may differ from a plain program's by a relative error of at most 0.023.
Values may be sent and summed in bfloat16 or wider, within the bound.
No kernel may reach another device: no remote copies, remote signals or barrier semaphores. Data moves between devices by JAX's collectives and lax.ppermute only.
A program may use at most 64 MiB of HBM per device.

v0:
```python
import math
import jax
import jax.numpy as jnp
from jax import lax
from jax.sharding import PartitionSpec as P

QH = 16
KVH = 4
HD = 64
PLEN = 4096
NEG_FILL = -1e30


def token_layout(lengths, total_rows):
    ends_at = jnp.cumsum(lengths)
    starts_at = ends_at - lengths
    indices = jnp.arange(total_rows, dtype=jnp.int32)
    request = jnp.sum((indices[:, None] >= ends_at[None, :]).astype(jnp.int32), axis=1)
    begins = jnp.max(
        jnp.where(starts_at[None, :] <= indices[:, None], starts_at[None, :], 0), axis=1
    )
    return ((PLEN + indices - begins).astype(jnp.float32), request)


def rope_tables(positions):
    halves = HD // 2
    steps_float = jnp.arange(halves, dtype=jnp.float32)
    inverse = jnp.exp(steps_float * (-2.0 * math.log(10000.0) / HD))
    angles = positions[:, None] * inverse[None, :]
    return (jnp.cos(angles), jnp.sin(angles))


def rotate(values, cos_table, sin_table):
    halves = values.shape[-1] // 2
    former = values[..., :halves]
    latter = values[..., halves:]
    cos_rows = cos_table[:, None, :]
    sin_rows = sin_table[:, None, :]
    return jnp.concatenate(
        [former * cos_rows - latter * sin_rows, latter * cos_rows + former * sin_rows], axis=-1
    )


def norm_rows(inputs):
    floats = inputs.astype(jnp.float32)
    return (floats * lax.rsqrt(jnp.mean(floats * floats, axis=-1, keepdims=True) + 1e-05)).astype(
        jnp.bfloat16
    )


def softmax_block(queries, keys_block, values_block, scaling, allowed):
    scores = (
        jnp.einsum("thd,nhd->thn", queries, keys_block, preferred_element_type=jnp.float32)
        * scaling
    )
    if allowed is not None:
        scores = jnp.where(allowed, scores, NEG_FILL)
    top_score = jnp.max(scores, axis=2)
    exponent = jnp.exp(scores - top_score[:, :, None])
    weight = jnp.sum(exponent, axis=2)
    blended = jnp.einsum(
        "thn,nhd->thd",
        exponent.astype(jnp.bfloat16),
        values_block,
        preferred_element_type=jnp.float32,
    )
    return (top_score, weight, blended)


def merge_states(former, latter):
    top_one, weight_one, blend_one = former
    top_two, weight_two, blend_two = latter
    overall = jnp.maximum(top_one, top_two)
    factor_one = jnp.exp(top_one - overall)
    factor_two = jnp.exp(top_two - overall)
    return (
        overall,
        weight_one * factor_one + weight_two * factor_two,
        blend_one * factor_one[:, :, None] + blend_two * factor_two[:, :, None],
    )


def on_device(
    tokens,
    lengths,
    group_prefix,
    prefix_cache,
    query_weight,
    key_weight,
    value_weight,
    out_weight,
    gate_up_weight,
    down_weight,
):
    tensor_count = lax.axis_size("tensor")
    tensor_rank = lax.axis_index("tensor")
    group_rank = lax.axis_index("dp")
    row_count = tokens.shape[0]
    group_tokens = row_count * tensor_count
    local_heads = query_weight.shape[1] // HD
    head_ratio = QH // KVH
    local_kv = max(1, local_heads // head_ratio)
    repeat_by = local_heads // local_kv
    kv_first = tensor_rank * local_heads // head_ratio
    kv_total = KVH * HD
    query_width = local_heads * HD
    kv_width = local_kv * HD
    scaling = 1.0 / math.sqrt(HD)
    positions, request = token_layout(lengths[0], group_tokens)
    cos_table, sin_table = rope_tables(positions)
    key_cols = lax.dynamic_slice_in_dim(key_weight, kv_first * HD, kv_width, 1)
    value_cols = lax.dynamic_slice_in_dim(value_weight, kv_first * HD, kv_width, 1)
    projection = jnp.concatenate([query_weight, key_cols, value_cols], axis=1)
    normed = norm_rows(tokens)
    segment = lax.all_gather(normed, "tensor", axis=0, tiled=True)
    seg_rows = segment.shape[0]
    mapped = jnp.dot(segment, projection, preferred_element_type=jnp.float32)
    query_part = rotate(
        mapped[:, :query_width].reshape(seg_rows, local_heads, HD), cos_table, sin_table
    )
    key_part = rotate(
        mapped[:, query_width : query_width + kv_width].reshape(seg_rows, local_kv, HD),
        cos_table,
        sin_table,
    )
    projected = jnp.concatenate(
        [
            query_part.reshape(seg_rows, query_width),
            key_part.reshape(seg_rows, kv_width),
            mapped[:, query_width + kv_width :],
        ],
        axis=1,
    ).astype(jnp.bfloat16)
    queries = projected[:, :query_width].reshape(group_tokens, local_heads, HD)
    own_keys = jnp.repeat(
        projected[:, query_width : query_width + kv_width].reshape(group_tokens, local_kv, HD),
        repeat_by,
        axis=1,
    )
    own_values = jnp.repeat(
        projected[:, query_width + kv_width :].reshape(group_tokens, local_kv, HD),
        repeat_by,
        axis=1,
    )
    slot_wanted = group_prefix[group_rank]
    shard_rows = prefix_cache.shape[0]
    segment = lax.all_gather(prefix_cache, "dp", axis=0, tiled=True)
    seg_rows = segment.shape[0]
    indices = jnp.arange(seg_rows, dtype=jnp.int32)
    matches = indices // shard_rows == slot_wanted
    places = indices % shard_rows
    chosen = (
        jnp.zeros_like(prefix_cache)
        .at[places]
        .add(jnp.where(matches[:, None], segment, jnp.zeros_like(segment)))
    )
    start_state = (
        jnp.full((group_tokens, local_heads), NEG_FILL, jnp.float32),
        jnp.zeros((group_tokens, local_heads), jnp.float32),
        jnp.zeros((group_tokens, local_heads, HD), jnp.float32),
    )
    segment = lax.all_gather(chosen, "tensor", axis=0, tiled=True)
    seg_rows = segment.shape[0]
    keys_block = lax.dynamic_slice_in_dim(segment, kv_first * HD, kv_width, 1).reshape(
        seg_rows, local_kv, HD
    )
    values_block = lax.dynamic_slice_in_dim(segment, kv_total + kv_first * HD, kv_width, 1).reshape(
        seg_rows, local_kv, HD
    )
    keys_block = jnp.repeat(keys_block, repeat_by, axis=1)
    values_block = jnp.repeat(values_block, repeat_by, axis=1)
    prefix_state = merge_states(
        start_state, softmax_block(queries, keys_block, values_block, scaling, None)
    )
    indices = jnp.arange(group_tokens, dtype=jnp.int32)
    allowed = (request[:, None] == request[None, :]) & (indices[None, :] <= indices[:, None])
    suffix_state = softmax_block(queries, own_keys, own_values, scaling, allowed[:, None, :])
    top_score, weight, blended = merge_states(prefix_state, suffix_state)
    attended = (
        (blended / weight[:, :, None]).astype(jnp.bfloat16).reshape(group_tokens, query_width)
    )
    attn_sum = lax.psum_scatter(
        jnp.dot(attended, out_weight, preferred_element_type=jnp.float32).astype(jnp.bfloat16),
        "tensor",
        scatter_dimension=0,
        tiled=True,
    ).astype(jnp.float32)
    middle = (tokens.astype(jnp.float32) + attn_sum).astype(jnp.bfloat16)
    segment = lax.all_gather(norm_rows(middle), "tensor", axis=0, tiled=True)
    gate_value = jnp.dot(segment, gate_up_weight[0], preferred_element_type=jnp.float32)
    upward = jnp.dot(segment, gate_up_weight[1], preferred_element_type=jnp.float32)
    hidden = (jax.nn.silu(gate_value) * upward).astype(jnp.bfloat16)
    ffn_sum = lax.psum_scatter(
        jnp.dot(hidden, down_weight, preferred_element_type=jnp.float32).astype(jnp.bfloat16),
        "tensor",
        scatter_dimension=0,
        tiled=True,
    ).astype(jnp.float32)
    return (middle.astype(jnp.float32) + ffn_sum).astype(jnp.bfloat16)


def solution(mesh):
    return jax.shard_map(
        on_device,
        mesh=mesh,
        in_specs=(
            P(("dp", "tensor"), None),
            P("dp", None),
            P(),
            P(("dp", "tensor"), None),
            P(None, "tensor"),
            P(),
            P(),
            P("tensor", None),
            P(None, None, "tensor"),
            P("tensor", None),
        ),
        out_specs=P(("dp", "tensor"), None),
        check_vma=False,
    )
```

profile of v0, /device:TPU:32, one launch (start us, length us, event | category | flops | bytes accessed | tf_op | source)
XLA Modules:
  0.0 400.2 jit_solution(4943395580398315689)
XLA Ops:
  6.5 0.7 all-gather.5.cloned.1.call-update
  7.3 1.0 fusion.66
  8.4 1.7 fusion.67
  10.1 0.0 all-gather.7.cloned.1.call-start
  10.1 1.2 dynamic_slice.15
  11.4 0.6 fusion.93
  12.0 41.6 %all-gather.5.cloned.1.call-done = bf16[4096,512]{1,0:T(8,128)(2,1)} async-done(((bf16[256,512]{1,0:T(8,128)(2,1)}), bf16[4096,512]{1,0:T(8,128)(2,1)}) %all-gather.5.cloned.1.call-update) | async-done | bytes 4194320 | tf_op jit(solution)/shard_map/all_gather | solution.py:147
  53.6 28.1 %scatter_custom_fusion = bf16[256,512]{1,0:T(8,128)(2,1)} fusion(s32[4096]{0:T(1024)S(1)} %bitcast.114, bf16[4096,512]{1,0:T(8,128)(2,1)} %all-gather.5.cloned.1.call-done, pred[4096]{0:T(1024)(128)(4,1)S(1)} %fusion.93, bf16[]{:T(256)} %constant.71.clone.1), kind=kCustom, calls=%fused_computation.7 | custom fusion | flops 4194304 | bytes 4461568 | tf_op jit(solution)/shard_map/scatter-add | solution.py:155
  81.9 0.2 reduce-window.4
  82.1 0.3 copy.13
  82.4 0.1 select_reduce_fusion
  82.5 0.1 convert_reduce_fusion
  82.5 1.6 constant_dynamic-slice_fusion
  84.1 20.8 %all-gather.9.cloned.1.call-done = bf16[512,2048]{1,0:T(8,128)(2,1)} async-done(((bf16[32,2048]{1,0:T(8,128)(2,1)}), bf16[512,2048]{1,0:T(8,128)(2,1)}) %all-gather.9.cloned.1.call-update) | async-done | bytes 2097168 | tf_op jit(solution)/shard_map/all_gather | solution.py:115
  104.9 2.7 fusion.41
  107.7 0.3 fusion.86
  108.0 0.4 fusion.112
  108.4 0.2 fusion.51
  108.6 54.8 %all-gather.7.cloned.1.call-done = bf16[4096,512]{1,0:T(8,128)(2,1)} async-done(((bf16[256,512]{1,0:T(8,128)(2,1)}), bf16[4096,512]{1,0:T(8,128)(2,1)}) %all-gather.7.cloned.1.call-update) | async-done | bytes 4194320 | tf_op jit(solution)/shard_map/all_gather | solution.py:162
  163.4 2.5 multiply_reduce_fusion
  165.9 1.4 fusion.1
  167.4 3.1 fusion.36
  170.5 2.3 convolution_convert_fusion.1
  172.9 79.3 %reduce-scatter.3.cloned.1.call-done = bf16[32,2048]{1,0:T(8,128)(2,1)} async-done(((bf16[512,2048]{1,0:T(8,128)(2,1)}), bf16[32,2048]{1,0:T(8,128)(2,1)}) %reduce-scatter.3.cloned.1.call-update) | async-done | bytes 131088 | tf_op jit(solution)/shard_map/reduce_scatter | solution.py:182
  252.2 1.1 fusion.69
  253.3 1.7 fusion.70
  255.0 0.2 reduce-scatter.5.cloned.1.call-start
  255.2 49.2 %all-gather.11.cloned.1.call-done = bf16[512,2048]{1,0:T(8,128)(2,1)} async-done(((bf16[32,2048]{1,0:T(8,128)(2,1)}), bf16[512,2048]{1,0:T(8,128)(2,1)}) %all-gather.11.cloned.1.call-update) | async-done | bytes 2097168 | tf_op jit(solution)/shard_map/all_gather | solution.py:189
  304.4 2.8 fusion.13
  307.2 5.5 %convolution_convert_fusion = bf16[512,2048]{1,0:T(8,128)(2,1)} fusion(bf16[320,2048]{1,0:T(8,128)(2,1)S(1)} %copy-done, bf16[512,2048]{1,0:T(8,128)(2,1)} %all-gather.11.cloned.1.call-done, bf16[2,2048,320]{1,2,0:T(8,128)(2,1)} %param.18, f32[512,320]{0,1:T(8,128)S(1)} %fusion.13), kind=kOutput, calls=%fused_computation.11 | convolution fusion | flops 1344208896 | bytes 7471104 | tf_op jit(solution)/shard_map/dot_general | solution.py:194
  312.7 79.0 %reduce-scatter.5.cloned.1.call-done = bf16[32,2048]{1,0:T(8,128)(2,1)} async-done(((bf16[512,2048]{1,0:T(8,128)(2,1)}), bf16[32,2048]{1,0:T(8,128)(2,1)}) %reduce-scatter.5.cloned.1.call-update) | async-done | bytes 131088 | tf_op jit(solution)/shard_map/reduce_scatter | solution.py:193
  391.7 1.6 fusion.71
  (29 shorter events, 0.3 us)
Async XLA Ops:
  6.5 300.7 %copy-start = (bf16[320,2048]{1,0:T(8,128)(2,1)S(1)}, bf16[320,2048]{1,0:T(8,128)(2,1)}, u32[]{:S(2)}) copy-start(bf16[320,2048]{1,0:T(8,128)(2,1)} %param.19) | copy-start | bytes 3932164
  6.5 47.1 %all-gather.5.cloned.1.call-start = ((), (), s32[]{:S(2)}) async-start(), calls=%async_computation.2 | async-start | bytes 4456448 | tf_op jit(solution)/shard_map/all_gather | solution.py:147
  7.3 97.7 %all-gather.9.cloned.1.call-start = ((), (), s32[]{:S(2)}) async-start(), calls=%async_computation.4 | async-start | bytes 2228224 | tf_op jit(solution)/shard_map/all_gather | solution.py:115
  8.3 73.5 %copy-start.5 = (s32[1,8]{1,0:T(1,128)S(1)}, s32[1,8]{1,0:T(1,128)}, u32[]{:S(2)}) copy-start(s32[1,8]{1,0:T(1,128)} %param.11) | copy-start | bytes 100
  8.4 73.7 %copy-start.3 = (bf16[2048,64]{0,1:T(8,128)(2,1)S(1)}, bf16[2048,64]{0,1:T(8,128)(2,1)}, u32[]{:S(2)}) copy-start(bf16[2048,64]{0,1:T(8,128)(2,1)} %param.14) | copy-start | bytes 786436
  10.1 153.3 %all-gather.7.cloned.1.call-start = ((), (), s32[]{:S(2)}) async-start(), calls=%async_computation.3 | async-start | bytes 4456448 | tf_op jit(solution)/shard_map/all_gather | solution.py:162
  81.8 170.5 %reduce-scatter.3.cloned.1.call-start = ((), (), s32[]{:S(2)}) async-start(), calls=%async_computation.5 | async-start | bytes 2228224 | tf_op jit(solution)/shard_map/reduce_scatter | solution.py:182
  167.4 3.1 copy-start.4
  170.5 81.7 %copy-start.1 = (bf16[32,2048]{1,0:T(8,128)(2,1)S(1)}, bf16[32,2048]{1,0:T(8,128)(2,1)}, u32[]{:S(2)}) copy-start(bf16[32,2048]{1,0:T(8,128)(2,1)} %param.10) | copy-start | bytes 393220
  172.9 131.5 %all-gather.11.cloned.1.call-start = ((), (), s32[]{:S(2)}) async-start(), calls=%async_computation.6 | async-start | bytes 2228224 | tf_op jit(solution)/shard_map/all_gather | solution.py:189
  255.0 136.8 %reduce-scatter.5.cloned.1.call-start = ((), (), s32[]{:S(2)}) async-start(), calls=%async_computation.7 | async-start | bytes 2228224 | tf_op jit(solution)/shard_map/reduce_scatter | solution.py:193
  307.2 84.5 %copy-start.2 = (bf16[32,2048]{1,0:T(8,128)(2,1)S(1)}, bf16[32,2048]{1,0:T(8,128)(2,1)}, u32[]{:S(2)}) copy-start(bf16[32,2048]{1,0:T(8,128)(2,1)} %reduce-scatter.3.cloned.1.call-done) | copy-start | bytes 393220
Sparse Core Ops, SparseCore 0:
  9.2 44.4 all-gather.4
  56.1 48.8 all-gather.8
  107.4 55.9 all-gather.6
  173.0 79.2 reduce-scatter.2
  255.1 49.2 all-gather.10
  312.9 78.8 reduce-scatter.4
where the time goes:
time: 401 us; the launch traced here: 400 us
  waiting for transfers between devices  325 us (81%)
  other arithmetic  38.2 us (10%)
  matrix products  19.4 us (5%)
  between operations  13.7 us (3%)
    reduce_scatter x1, waiting for transfers between devices, on_device(): lax.psum_scatter(jnp.dot(attended, out_weight, preferred_element_type=jnp...  79.3 us
    reduce_scatter x1, waiting for transfers between devices, on_device(): lax.psum_scatter(jnp.dot(hidden, down_weight, preferred_element_type=jnp....  79 us
    all_gather x1, waiting for transfers between devices, on_device(): segment = lax.all_gather(chosen, 'tensor', axis=0, tiled=True)  54.8 us
    all_gather x1, waiting for transfers between devices, on_device(): segment = lax.all_gather(norm_rows(middle), 'tensor', axis=0, tiled=True)  49.2 us
    all_gather x1, waiting for transfers between devices, on_device(): segment = lax.all_gather(prefix_cache, 'dp', axis=0, tiled=True)  41.6 us
    scatter-add x1, other arithmetic, on_device(): chosen = jnp.zeros_like(prefix_cache).at[places].add(jnp.where(matches[:,...  28.1 us
    all_gather x1, waiting for transfers between devices, on_device(): segment = lax.all_gather(normed, 'tensor', axis=0, tiled=True)  20.8 us
  transfers between devices with their start and end apart: 6, of which 6 were waited for; matrix products, arithmetic and copies ran while one was open for 10% of the time, Pallas kernels for 0%

commit v1 on v0

--- a/solution.py
+++ b/solution.py
@@ -112,7 +112,9 @@
     value_cols = lax.dynamic_slice_in_dim(value_weight, kv_first * HD, kv_width, 1)
     projection = jnp.concatenate([query_weight, key_cols, value_cols], axis=1)
     normed = norm_rows(tokens)
-    segment = lax.all_gather(normed, "tensor", axis=0, tiled=True)
+    segment = jnp.concatenate(
+        lax.all_to_all(jnp.stack([normed] * lax.axis_size("tensor")), "tensor", 0, 0), axis=0
+    )
     seg_rows = segment.shape[0]
     mapped = jnp.dot(segment, projection, preferred_element_type=jnp.float32)
     query_part = rotate(

time: 401 us -> 389 us (0.970)
  waiting for transfers between devices: 325 us -> 308 us
  starting transfers between devices: 0.39 us -> 7.34 us
    all_to_all x0 -> x1, waiting for transfers between devices: none -> 34.6 us  [on_device(): lax.all_to_all(jnp.stack([normed] * lax.axis_size('tensor')), 'tensor', 0...]
    all_gather x1, waiting for transfers between devices: 54.8 us -> 20.7 us  [on_device(): segment = lax.all_gather(chosen, 'tensor', axis=0, tiled=True)]
    all_gather x1 -> x0, waiting for transfers between devices: 20.8 us -> none  [on_device(): segment = lax.all_gather(normed, 'tensor', axis=0, tiled=True)]
    all_to_all x0 -> x1, starting transfers between devices: none -> 6.99 us  [on_device(): lax.all_to_all(jnp.stack([normed] * lax.axis_size('tensor')), 'tensor', 0...]
  transfers between devices with their start and end apart: 6 -> 6, of which waited for: 6 -> 6; matrix products, arithmetic and copies ran while one was open for 10% -> 2% of each run, Pallas kernels for 0% -> 0%
where the time goes in v1:
time: 389 us; the launch traced here: 388 us
  waiting for transfers between devices  308 us (79%)
  other arithmetic  35.7 us (9%)
  matrix products  19.4 us (5%)
  between operations  13.3 us (3%)
  starting transfers between devices  7.34 us (2%)
  local copies, waits for them, and re-layouts  4.72 us (1%)
    reduce_scatter x1, waiting for transfers between devices, on_device(): lax.psum_scatter(jnp.dot(attended, out_weight, preferred_element_type=jnp...  79.2 us
    reduce_scatter x1, waiting for transfers between devices, on_device(): lax.psum_scatter(jnp.dot(hidden, down_weight, preferred_element_type=jnp....  78.9 us
    all_gather x1, waiting for transfers between devices, on_device(): segment = lax.all_gather(norm_rows(middle), 'tensor', axis=0, tiled=True)  49.2 us
    all_gather x1, waiting for transfers between devices, on_device(): segment = lax.all_gather(prefix_cache, 'dp', axis=0, tiled=True)  44.4 us
    all_to_all x1, waiting for transfers between devices, on_device(): lax.all_to_all(jnp.stack([normed] * lax.axis_size('tensor')), 'tensor', 0...  34.6 us
    scatter-add x1, other arithmetic, on_device(): chosen = jnp.zeros_like(prefix_cache).at[places].add(jnp.where(matches[:,...  28.1 us
    all_gather x1, waiting for transfers between devices, on_device(): segment = lax.all_gather(chosen, 'tensor', axis=0, tiled=True)  20.7 us
  transfers between devices with their start and end apart: 6, of which 6 were waited for; matrix products, arithmetic and copies ran while one was open for 2% of the time, Pallas kernels for 0%

profile of v1, /device:TPU:32, one launch (start us, length us, event | category | flops | bytes accessed | tf_op | source)
XLA Modules:
  0.0 388.3 jit_solution(10369378314448828358)
XLA Ops:
  6.5 0.7 all-gather.4.cloned.1.call-update
  7.3 1.2 dynamic_slice.15
  8.6 0.7 fusion.93
  9.2 44.4 %all-gather.4.cloned.1.call-done = bf16[4096,512]{1,0:T(8,128)(2,1)} async-done(((bf16[256,512]{1,0:T(8,128)(2,1)}), bf16[4096,512]{1,0:T(8,128)(2,1)}) %all-gather.4.cloned.1.call-update) | async-done | bytes 4194320 | tf_op jit(solution)/shard_map/all_gather | solution.py:149
  53.6 28.1 %scatter_custom_fusion = bf16[256,512]{1,0:T(8,128)(2,1)} fusion(s32[4096]{0:T(1024)S(1)} %bitcast.115, bf16[4096,512]{1,0:T(8,128)(2,1)} %all-gather.4.cloned.1.call-done, pred[4096]{0:T(1024)(128)(4,1)S(1)} %fusion.93, bf16[]{:T(256)} %constant.71.clone.1), kind=kCustom, calls=%fused_computation.7 | custom fusion | flops 4194304 | bytes 4461568 | tf_op jit(solution)/shard_map/scatter-add | solution.py:157
  81.8 0.1 fusion.66
  81.9 0.1 fusion.67
  82.1 1.6 stack.2
  83.7 7.0 %all-to-all-start = ((bf16[16,32,2048]{2,1,0:T(8,128)(2,1)}), bf16[16,32,2048]{2,1,0:T(8,128)(2,1)}, u32[]{:S(2)}, u32[]{:S(2)}) async-start(bf16[16,32,2048]{2,1,0:T(8,128)(2,1)} %stack.2), calls=%async_computation | async-start | bytes 4194304 | tf_op jit(solution)/shard_map/all_to_all | solution.py:116
  90.7 0.2 reduce-window.4
  90.9 0.3 copy.13
  91.2 0.1 select_reduce_fusion
  91.4 1.6 constant_dynamic-slice_fusion
  93.0 34.6 %all-to-all-done = bf16[16,32,2048]{2,1,0:T(8,128)(2,1)} async-done(((bf16[16,32,2048]{2,1,0:T(8,128)(2,1)}), bf16[16,32,2048]{2,1,0:T(8,128)(2,1)}, u32[]{:S(2)}, u32[]{:S(2)}) %all-to-all-start) | async-done | bytes 2097184 | tf_op jit(solution)/shard_map/all_to_all | solution.py:116
  127.6 2.7 fusion.41
  130.3 0.3 fusion.86
  130.7 0.4 fusion.112
  131.1 0.2 fusion.51
  131.3 20.7 %all-gather.6.cloned.1.call-done = bf16[4096,512]{1,0:T(8,128)(2,1)} async-done(((bf16[256,512]{1,0:T(8,128)(2,1)}), bf16[4096,512]{1,0:T(8,128)(2,1)}) %all-gather.6.cloned.1.call-update) | async-done | bytes 4194320 | tf_op jit(solution)/shard_map/all_gather | solution.py:164
  152.0 2.5 multiply_reduce_fusion
  154.5 1.4 fusion.1
  156.0 3.1 fusion.36
  159.1 2.3 convolution_convert_fusion.1
  161.5 79.2 %reduce-scatter.3.cloned.1.call-done = bf16[32,2048]{1,0:T(8,128)(2,1)} async-done(((bf16[512,2048]{1,0:T(8,128)(2,1)}), bf16[32,2048]{1,0:T(8,128)(2,1)}) %reduce-scatter.3.cloned.1.call-update) | async-done | bytes 131088 | tf_op jit(solution)/shard_map/reduce_scatter | solution.py:184
  240.7 1.1 fusion.69
  241.8 1.7 fusion.70
  243.5 0.2 reduce-scatter.5.cloned.1.call-start
  243.7 49.2 %all-gather.8.cloned.1.call-done = bf16[512,2048]{1,0:T(8,128)(2,1)} async-done(((bf16[32,2048]{1,0:T(8,128)(2,1)}), bf16[512,2048]{1,0:T(8,128)(2,1)}) %all-gather.8.cloned.1.call-update) | async-done | bytes 2097168 | tf_op jit(solution)/shard_map/all_gather | solution.py:191
  292.9 2.8 fusion.13
  295.7 5.5 %convolution_convert_fusion = bf16[512,2048]{1,0:T(8,128)(2,1)} fusion(bf16[320,2048]{1,0:T(8,128)(2,1)S(1)} %copy-done, bf16[512,2048]{1,0:T(8,128)(2,1)} %all-gather.8.cloned.1.call-done, bf16[2,2048,320]{1,2,0:T(8,128)(2,1)} %param.18, f32[512,320]{0,1:T(8,128)S(1)} %fusion.13), kind=kOutput, calls=%fused_computation.11 | convolution fusion | flops 1344208896 | bytes 7471104 | tf_op jit(solution)/shard_map/dot_general | solution.py:196
  301.2 78.9 %reduce-scatter.5.cloned.1.call-done = bf16[32,2048]{1,0:T(8,128)(2,1)} async-done(((bf16[512,2048]{1,0:T(8,128)(2,1)}), bf16[32,2048]{1,0:T(8,128)(2,1)}) %reduce-scatter.5.cloned.1.call-update) | async-done | bytes 131088 | tf_op jit(solution)/shard_map/reduce_scatter | solution.py:195
  380.2 1.6 fusion.71
  (29 shorter events, 0.4 us)
Async XLA Ops:
  6.5 289.2 %copy-start = (bf16[320,2048]{1,0:T(8,128)(2,1)S(1)}, bf16[320,2048]{1,0:T(8,128)(2,1)}, u32[]{:S(2)}) copy-start(bf16[320,2048]{1,0:T(8,128)(2,1)} %param.19) | copy-start | bytes 3932164
  6.5 75.3 %copy-start.1 = (bf16[32,2048]{1,0:T(8,128)(2,1)S(1)}, bf16[32,2048]{1,0:T(8,128)(2,1)}, u32[]{:S(2)}) copy-start(bf16[32,2048]{1,0:T(8,128)(2,1)} %param.10) | copy-start | bytes 393220
  6.5 47.1 %all-gather.4.cloned.1.call-start = ((), (), s32[]{:S(2)}) async-start(), calls=%async_computation.3 | async-start | bytes 4456448 | tf_op jit(solution)/shard_map/all_gather | solution.py:149
  7.3 144.7 %all-gather.6.cloned.1.call-start = ((), (), s32[]{:S(2)}) async-start(), calls=%async_computation.4 | async-start | bytes 4456448 | tf_op jit(solution)/shard_map/all_gather | solution.py:164
  83.7 7.1 %copy-start.5 = (s32[1,8]{1,0:T(1,128)S(1)}, s32[1,8]{1,0:T(1,128)}, u32[]{:S(2)}) copy-start(s32[1,8]{1,0:T(1,128)} %param.11) | copy-start | bytes 100
  83.7 7.3 %copy-start.3 = (bf16[2048,64]{0,1:T(8,128)(2,1)S(1)}, bf16[2048,64]{0,1:T(8,128)(2,1)}, u32[]{:S(2)}) copy-start(bf16[2048,64]{0,1:T(8,128)(2,1)} %param.14) | copy-start | bytes 786436
  83.7 43.9 %all-to-all-start = ((bf16[16,32,2048]{2,1,0:T(8,128)(2,1)}), bf16[16,32,2048]{2,1,0:T(8,128)(2,1)}, u32[]{:S(2)}, u32[]{:S(2)}) async-start(bf16[16,32,2048]{2,1,0:T(8,128)(2,1)} %stack.2), calls=%async_computation | async-start | bytes 4194304 | tf_op jit(solution)/shard_map/all_to_all | solution.py:116
  90.7 150.1 %reduce-scatter.3.cloned.1.call-start = ((), (), s32[]{:S(2)}) async-start(), calls=%async_computation.5 | async-start | bytes 2228224 | tf_op jit(solution)/shard_map/reduce_scatter | solution.py:184
  156.0 3.1 copy-start.4
  161.4 131.4 %all-gather.8.cloned.1.call-start = ((), (), s32[]{:S(2)}) async-start(), calls=%async_computation.6 | async-start | bytes 2228224 | tf_op jit(solution)/shard_map/all_gather | solution.py:191
  243.5 136.7 %reduce-scatter.5.cloned.1.call-start = ((), (), s32[]{:S(2)}) async-start(), calls=%async_computation.7 | async-start | bytes 2228224 | tf_op jit(solution)/shard_map/reduce_scatter | solution.py:195
  295.7 84.4 %copy-start.2 = (bf16[32,2048]{1,0:T(8,128)(2,1)S(1)}, bf16[32,2048]{1,0:T(8,128)(2,1)}, u32[]{:S(2)}) copy-start(bf16[32,2048]{1,0:T(8,128)(2,1)} %reduce-scatter.3.cloned.1.call-done) | copy-start | bytes 393220
Sparse Core Ops, SparseCore 0:
  9.2 44.4 all-gather.3
  81.9 70.0 all-gather.5
  161.6 79.1 reduce-scatter.2
  243.6 49.2 all-gather.7
  301.4 78.7 reduce-scatter.4
